TPU v7x, 128 devices: a whole 4x4x4 slice. The times are simulated.
128 devices in a mesh: child: 2 (over z_hi), row: 8 (over y, core), col: 8 (over x, z_lo).
Axes of the slice: x: 4, y: 4, z: 4 (z_hi: 2, z_lo: 2; z = z_hi * 2 + z_lo), core: 2. Of those that a mesh axis runs over, the one named last changes fastest.
Arguments:
- child_fronts: float32 [2, 8192, 8192], P('child', 'row', 'col')
- parent_front: float32 [12288, 12288], P('row', ('child', 'col')), may hold values from -6 to 6
- index_maps: int32 [2, 8192], replicated, may hold values from 0 to 12287, as said below
- orders: int32 [2], replicated, may hold values from 4096 to 8192, as said below
Outputs:
- assembled: float32 [12288, 12288], P('row', ('child', 'col'))
- panel_factor: float32 [2, 8192, 512], P('child', 'row')
Inputs may be any that keep to these rules, and one draw needn't show every extreme that they name: For each child, index_maps is one to one. Cut the child indices into aligned blocks of 8192 / 8 and the parent indices into 2 * 8 aligned slices of 12288 / (2 * 8): each block sends exactly 8192 / (2 * 8 * 8) of its indices into each slice. `orders`: one child's order is 8192.
All inputs are finite; a program needn't handle non-finite values.
Results may differ from a plain program's by a relative error of at most 0.0001.
Values sent between devices are 32-bit elements; how exact they have to be, the bound alone decides.
No kernel may reach another device: no remote copies, remote signals or barrier semaphores. Data moves between devices by JAX's collectives and lax.ppermute only.
A program may use at most 128 MiB of HBM per device.

v0:
```python
import jax
import jax.numpy as jnp
from jax import lax
from jax.sharding import PartitionSpec as P

PANEL = 512
FRONT = 8192


def from_root(value, axis, source):
    kept = jnp.where(lax.axis_index(axis) == source, value, 0).astype(value.dtype)
    return lax.psum(kept, axis)


def spread_sum(value, axis):
    count = lax.axis_size(axis)
    pieces = value.reshape(count, value.shape[0] // count, value.shape[1])
    arrived = lax.all_to_all(pieces, axis, 0, 0, tiled=True)
    return lax.all_gather(arrived.sum(0), axis, axis=0, tiled=True)


def from_first(value, axis, gather=True):
    count = lax.axis_size(axis)
    pieces = value.reshape(count, value.shape[0] // count, value.shape[1])
    arrived = lax.all_to_all(pieces, axis, 0, 0, tiled=True)
    if not gather:
        return arrived[0]
    return lax.all_gather(arrived[0], axis, axis=0, tiled=True)


def select_rows(parent_map, owner, width, count):
    everywhere = jnp.arange(FRONT, dtype=jnp.int32)
    keyed = jnp.where(parent_map // width == owner, everywhere, everywhere + FRONT)
    chosen = jnp.argsort(keyed)[:count]
    return parent_map[chosen] - owner * width


def invert_slots(slots, length):
    count = slots.shape[0]
    lookup = jnp.full((length,), count, jnp.int32)
    return lookup.at[slots].set(jnp.arange(count, dtype=jnp.int32))


def one_hot(order, size):
    positions = jnp.arange(size, dtype=jnp.int32)
    return (positions[:, None] == order[None, :]).astype(jnp.float32)


def exact_matmul(values, select):
    return jnp.dot(values, select, precision=lax.Precision.HIGHEST)


def factor_and_invert(matrix, size):
    count = matrix.shape[0] // size
    eye = jnp.eye(size, dtype=jnp.float32)
    high = lax.Precision.HIGHEST
    trailing = (matrix + matrix.T) * 0.5
    factor, inverse = ({}, {})
    for k in range(count):
        factor[k, k] = jnp.linalg.cholesky(trailing[:size, :size])
        inverse[k, k] = lax.linalg.triangular_solve(factor[k, k], eye, left_side=True, lower=True)
        if k + 1 < count:
            panel = jnp.dot(trailing[size:, :size], inverse[k, k].T, precision=high)
            for i in range(k + 1, count):
                factor[i, k] = panel[(i - k - 1) * size : (i - k) * size]
            trailing = trailing[size:, size:] - jnp.dot(panel, panel.T, precision=high)
    for i in range(count):
        for j in range(i - 1, -1, -1):
            total = sum((jnp.dot(factor[i, k], inverse[k, j], precision=high) for k in range(j, i)))
            inverse[i, j] = -jnp.dot(inverse[i, i], total, precision=high)
    zero = jnp.zeros((size, size), jnp.float32)

    def assemble(blocks):
        return jnp.concatenate(
            [
                jnp.concatenate([blocks[i, j] if j <= i else zero for j in range(count)], axis=1)
                for i in range(count)
            ]
        )

    return (assemble(factor), assemble(inverse))


def factor_panel(diag_factor, inverse, columns, global_rows, own_order):
    solved = jnp.dot(columns, inverse.T, precision=lax.Precision.HIGHEST)
    top_rows = jnp.pad(diag_factor, ((0, columns.shape[0] - PANEL), (0, 0)))
    result = jnp.where(global_rows[:, None] < PANEL, top_rows, solved)
    return jnp.where(global_rows[:, None] < own_order, result, jnp.float32(0.0))


def on_device(child_fronts, parent_front, index_maps, orders):
    block_here = child_fronts[0]
    rows_here, cols_here = block_here.shape
    child_index = lax.axis_index("child")
    row_index = lax.axis_index("row")
    col_index = lax.axis_index("col")
    n_row = lax.axis_size("row")
    n_col = lax.axis_size("col")
    own_map = lax.dynamic_index_in_dim(index_maps, child_index, 0, keepdims=False)
    own_order = lax.dynamic_index_in_dim(orders, child_index, 0, keepdims=False)
    global_rows = row_index * rows_here + jnp.arange(rows_here, dtype=jnp.int32)
    global_cols = col_index * cols_here + jnp.arange(cols_here, dtype=jnp.int32)
    panel_rows = rows_here // n_col
    first_piece = block_here[:panel_rows, :PANEL]
    for target in range(1, n_col):
        moved = lax.ppermute(
            block_here[target * panel_rows : (target + 1) * panel_rows, :PANEL],
            "col",
            [(0, target)],
        )
        first_piece = jnp.where(col_index == target, moved, first_piece)
    columns = lax.all_gather(first_piece, "col", axis=0, tiled=True)
    part_rows = rows_here // n_row
    own_piece = lax.dynamic_slice_in_dim(columns, col_index * part_rows, part_rows)
    pairs = [(n_col * a + b, n_col * b + a) for a in range(n_row) for b in range(n_col)]
    transposed_piece = lax.ppermute(own_piece, ("row", "col"), pairs)
    corner_rows = PANEL // n_row
    corner_piece = columns[:corner_rows]
    for target in range(1, n_row):
        moved = lax.ppermute(
            columns[target * corner_rows : (target + 1) * corner_rows], "row", [(0, target)]
        )
        corner_piece = jnp.where(row_index == target, moved, corner_piece)
    gathered = lax.all_gather(
        jnp.concatenate([transposed_piece, corner_piece]), "row", axis=0, tiled=False
    )
    other_columns = gathered[:, :part_rows].reshape(rows_here, PANEL)
    corner = gathered[:, part_rows:].reshape(PANEL, PANEL)
    diag_factor, inverse = factor_and_invert(corner, PANEL // 4)
    own_panel = factor_panel(diag_factor, inverse, columns, global_rows, own_order)
    other_panel = factor_panel(diag_factor, inverse, other_columns, global_cols, own_order)
    parent_rows, parent_cols = parent_front.shape
    row_map = lax.dynamic_slice_in_dim(own_map, row_index * rows_here, rows_here)
    col_map = lax.dynamic_slice_in_dim(own_map, col_index * cols_here, cols_here)
    row_keys = row_map // parent_rows * rows_here + jnp.arange(rows_here, dtype=jnp.int32)
    col_keys = col_map // parent_cols * cols_here + jnp.arange(cols_here, dtype=jnp.int32)
    col_order = jnp.argsort(col_keys)
    col_select = one_hot(col_order, cols_here)
    row_order = jnp.argsort(row_keys)
    live_rows = (global_rows >= PANEL) & (global_rows < own_order)
    live_cols = (global_cols >= PANEL) & (global_cols < own_order)
    update = block_here[row_order] - jnp.dot(
        own_panel[row_order], other_panel.T, precision=lax.Precision.HIGHEST
    )
    update = jnp.where(live_rows[row_order][:, None] & live_cols[None, :], update, jnp.float32(0.0))
    turned = jnp.einsum("qj,iq->ji", col_select, update, precision=lax.Precision.HIGHEST)
    part_cols = cols_here // (2 * n_col)
    pieces = (
        turned.reshape(2, n_col, part_cols, n_row, part_rows)
        .transpose(0, 3, 1, 2, 4)
        .reshape(-1, part_rows)
    )
    arrived = lax.all_to_all(
        pieces, ("child", "row", "col"), split_axis=0, concat_axis=0, tiled=True
    )
    arrived = arrived.reshape(2, n_row, n_col * part_cols, part_rows)
    col_owner = child_index * n_col + col_index
    assembled = parent_front
    for source in range(2):
        parent_map = index_maps[source]
        row_slots = select_rows(parent_map, row_index, parent_rows, rows_here)
        col_slots = select_rows(parent_map, col_owner, parent_cols, n_col * part_cols)
        row_lookup = invert_slots(row_slots, parent_rows)
        spread = jnp.einsum(
            "rqa,pq->rap",
            arrived[source],
            one_hot(col_slots, parent_cols),
            precision=lax.Precision.HIGHEST,
        ).reshape(rows_here, parent_cols)
        padded = jnp.pad(spread, ((0, 1), (0, 0)))
        assembled = assembled + jnp.take(padded, row_lookup, axis=0)
    return (assembled, own_panel[None])


def solution(mesh):
    in_specs = (P("child", "row", "col"), P("row", ("child", "col")), P(), P())
    out_specs = (P("row", ("child", "col")), P("child", "row", None))
    return jax.shard_map(
        on_device, mesh=mesh, in_specs=in_specs, out_specs=out_specs, check_vma=False
    )
```

profile of v0, /device:TPU:1, one launch (start us, length us, event | category | flops | bytes accessed | tf_op | source)
XLA Modules:
  0.0 416.2 jit_solution(1546975868611364427)
XLA Ops:
  8.8 4.4 %collective-permute-start.6 = (f32[128,512]{1,0:T(8,128)S(1)}, f32[128,512]{1,0:T(8,128)S(1)}, u32[]{:S(2)}, u32[]{:S(2)}) collective-permute-start(f32[128,512]{1,0:T(8,128)S(1)} %get-tuple-element.29), channel_id=1, source_target_pairs={{0,1},{8,9},{16,17},{24,25},{32,33},{40,41},{48,49},{56,57},{64,65... | collective-permute-start | bytes 786440 | tf_op jit(solution)/shard_map/ppermute | solution.py:106
  25.1 5.6 %collective-permute-done.3 = f32[128,512]{1,0:T(8,128)S(1)} collective-permute-done((f32[128,512]{1,0:T(8,128)S(1)}, f32[128,512]{1,0:T(8,128)S(1)}, u32[]{:S(2)}, u32[]{:S(2)}) %collective-permute-start.3) | collective-permute-done | bytes 262176 | tf_op jit(solution)/shard_map/ppermute | solution.py:106
  30.7 5.6 %collective-permute-done.2 = f32[128,512]{1,0:T(8,128)S(1)} collective-permute-done((f32[128,512]{1,0:T(8,128)S(1)}, f32[128,512]{1,0:T(8,128)S(1)}, u32[]{:S(2)}, u32[]{:S(2)}) %collective-permute-start.2) | collective-permute-done | bytes 262176 | tf_op jit(solution)/shard_map/ppermute | solution.py:106
  38.3 53.1 %all-gather.4.cloned.1.call-done = f32[1024,512]{1,0:T(8,128)} async-done(((f32[128,512]{1,0:T(8,128)}), f32[1024,512]{1,0:T(8,128)}) %all-gather.4.cloned.1.call-update) | async-done | bytes 2097168 | tf_op jit(solution)/shard_map/all_gather | solution.py:112
  99.8 10.2 %collective-permute-start.7 = (f32[128,512]{1,0:T(8,128)S(1)}, f32[128,512]{1,0:T(8,128)S(1)}, u32[]{:S(2)}, u32[]{:S(2)}) collective-permute-start(f32[128,512]{1,0:T(8,128)S(1)} %constant_dynamic-slice_fusion), channel_id=1, source_target_pairs={{0,0},{1,8},{2,16},{3,24},{4,32},{5,40},{6,48},{7,56},{8,1},{9,9},... | collective-permute-start | bytes 786440 | tf_op jit(solution)/shard_map/ppermute | solution.py:116
  121.7 8.5 %gather_fusion.1 = f32[1024,1024]{1,0:T(8,128)} fusion(f32[1024,1024]{1,0:T(8,128)} %bitcast.119, s32[1024]{0:T(1024)S(1)} %fusion.78), kind=kCustom, calls=%fused_computation.3 | custom fusion | bytes 8392704 | tf_op jit(solution)/shard_map/gather | solution.py:142
  130.8 7.0 %gather_fusion = pred[1024]{0:T(1024)(128)(4,1)S(1)} fusion(pred[1024]{0:T(1024)(128)(4,1)S(1)} %fusion.91, s32[1024]{0:T(1024)S(1)} %fusion.78), kind=kCustom, calls=%fused_computation.2 | custom fusion | bytes 6144 | tf_op jit(solution)/shard_map/gather | solution.py:145
  137.9 4.4 %sort.90 = (s32[1024]{0:T(1024)}, s32[1024]{0:T(1024)}) sort(s32[1024]{0:T(1024)S(1)} %get-tuple-element.62, s32[1024]{0:T(1024)S(1)} %iota.129), dimensions={0}, to_apply=%region_0.1 | sort | flops 10240 | bytes 16384 | tf_op jit(solution)/shard_map/jit(argsort)/sort | solution.py:137
  145.2 6.1 %all-gather.6.cloned.1.call-done = f32[1536,512]{1,0:T(8,128)} async-done(((f32[192,512]{1,0:T(8,128)}), f32[1536,512]{1,0:T(8,128)}) %all-gather.6.cloned.1.call-update) | async-done | bytes 3145744 | tf_op jit(solution)/shard_map/all_gather | solution.py:124
  156.5 11.7 %cholesky.74 = f32[128,128]{1,0:T(8,128)S(1)} custom-call(f32[128,128]{1,0:T(8,128)S(1)} %fusion.64), custom_call_target="Cholesky" | custom-call | tf_op jit(solution)/shard_map/jit(cholesky)/cholesky | solution.py:60
  169.7 9.8 %custom-call.8 = f32[1,128,128]{1,2,0:T(8,128)S(1)} custom-call(f32[1,128,128]{2,1,0:T(8,128)S(1)} %get-tuple-element.25), custom_call_target="InvertDiagBlocksLowerTriangular" | custom-call | tf_op jit(solution)/shard_map/triangular_solve/custom-call.0 | solution.py:61
  181.8 12.1 %cholesky.85 = f32[128,128]{1,0:T(8,128)S(1)} custom-call(f32[128,128]{1,0:T(8,128)S(1)} %fusion.62), custom_call_target="Cholesky" | custom-call | tf_op jit(solution)/shard_map/jit(cholesky)/cholesky | solution.py:60
  196.0 9.8 %custom-call.9 = f32[1,128,128]{1,2,0:T(8,128)S(1)} custom-call(f32[1,128,128]{2,1,0:T(8,128)S(1)} %get-tuple-element.23), custom_call_target="InvertDiagBlocksLowerTriangular" | custom-call | tf_op jit(solution)/shard_map/triangular_solve/custom-call.0 | solution.py:61
  207.7 11.7 %cholesky.96 = f32[128,128]{1,0:T(8,128)S(1)} custom-call(f32[128,128]{1,0:T(8,128)S(1)} %fusion.60), custom_call_target="Cholesky" | custom-call | tf_op jit(solution)/shard_map/jit(cholesky)/cholesky | solution.py:60
  221.3 9.8 %custom-call.10 = f32[1,128,128]{1,2,0:T(8,128)S(1)} custom-call(f32[1,128,128]{2,1,0:T(8,128)S(1)} %get-tuple-element.21), custom_call_target="InvertDiagBlocksLowerTriangular" | custom-call | tf_op jit(solution)/shard_map/triangular_solve/custom-call.0 | solution.py:61
  237.8 11.9 %cholesky.107 = f32[128,128]{1,0:T(8,128)S(1)} custom-call(f32[128,128]{1,0:T(8,128)S(1)} %fusion.58), custom_call_target="Cholesky" | custom-call | tf_op jit(solution)/shard_map/jit(cholesky)/cholesky | solution.py:60
  251.1 9.8 %custom-call.11 = f32[1,128,128]{1,2,0:T(8,128)S(1)} custom-call(f32[1,128,128]{2,1,0:T(8,128)S(1)} %get-tuple-element.19), custom_call_target="InvertDiagBlocksLowerTriangular" | custom-call | tf_op jit(solution)/shard_map/triangular_solve/custom-call.0 | solution.py:61
  264.7 5.8 %fusion.107 = f32[1024,512]{1,0:T(8,128)} fusion(f32[1024,512]{1,0:T(8,128)S(1)} %bitcast.130, f32[128,256]{1,0:T(8,128)S(1)} %broadcast.199, f32[128,128]{1,0:T(8,128)S(1)} %cholesky.75, f32[128,128]{1,0:T(8,128)S(1)} %fusion.45, f32[128,128]{1,0:T(8,128)S(1)} %copy.51, f32[128,128]{1,0:T(8,128)S(1)} %convolution_negate_fusion, ...), kind=kOutput, calls=%fused_computation.207 | convolution fusion | flops 3224633344 | bytes 5046272 | tf_op jit(solution)/shard_map/dot_general | solution.py:85
  270.8 4.9 %fusion.8 = f32[1024,512]{1,0:T(8,128)S(1)} fusion(f32[512,512]{1,0:T(8,128)S(1)} %fusion.21, f32[1024,512]{1,0:T(8,128)S(1)} %copy-done.4, pred[1024]{0:T(1024)(128)(4,1)S(1)} %copy-done.20, pred[1024]{0:T(1024)(128)(4,1)S(1)} %copy-done.21, f32[128,256]{1,0:T(8,128)S(1)} %broadcast.199, f32[128,128]{1,0:T(8,128)S(1)} %cholesky.75, ...), kind=kOutput, calls=%fused_computation.22 | convolution fusion | flops 3225681920 | bytes 6096896 | tf_op jit(solution)/shard_map/dot_general | solution.py:85
  275.7 4.9 %gather_fusion.2 = f32[1024,512]{1,0:T(8,128)} fusion(f32[1024,512]{1,0:T(8,128)S(1)} %fusion.8, s32[1024]{0:T(1024)S(1)} %fusion.78), kind=kCustom, calls=%fused_computation.4 | custom fusion | bytes 4198400 | tf_op jit(solution)/shard_map/gather | solution.py:143
  280.6 9.8 %fusion.10 = f32[1024,1024]{1,0:T(8,128)S(1)} fusion(f32[1024,512]{1,0:T(8,128)} %gather_fusion.2, f32[1024,512]{1,0:T(8,128)} %fusion.107, f32[512,512]{1,0:T(8,128)S(1)} %fusion.21, pred[1024]{0:T(1024)(128)(4,1)S(1)} %get-tuple-element.56, pred[1024]{0:T(1024)(128)(4,1)S(1)} %get-tuple-element.57), kind=kOutput, calls=%fused_computation.24 | convolution fusion | flops 6443499520 | bytes 9439232 | tf_op jit(solution)/shard_map/dot_general | solution.py:142
  290.5 9.0 %fusion.5 = f32[128,8,8,128]{3,1,2,0:T(8,128)S(1)} fusion(f32[1024,1024]{1,0:T(8,128)S(1)} %copy-done.2, f32[1024,1024]{1,0:T(8,128)S(1)} %fusion.10, s32[1024]{0:T(1024)S(1)} %copy-done.23, pred[1024]{0:T(1024)(128)(4,1)S(1)} %copy-done.22, pred[1024]{0:T(1024)(128)(4,1)S(1)} %gather_fusion), kind=kOutput, calls=%fused_computation.21 | convolution fusion | flops 12890144768 | bytes 12589056 | tf_op jit(solution)/shard_map/qj,iq->ji/dot_general | solution.py:146
  303.4 10.9 %all-to-all-start = ((f32[128,64,128]{2,1,0:T(8,128)}), f32[128,64,128]{2,1,0:T(8,128)}, u32[]{:S(2)}, u32[]{:S(2)}) async-start(f32[128,64,128]{2,1,0:T(8,128)} %bitcast.121), calls=%async_computation | async-start | bytes 8388608 | tf_op jit(solution)/shard_map/all_to_all | solution.py:153
  314.5 6.8 %sort.95 = (s32[8192]{0:T(1024)}, s32[8192]{0:T(1024)S(1)}) sort(s32[8192]{0:T(1024)S(1)} %get-tuple-element.54, s32[8192]{0:T(1024)S(1)} %iota.145), dimensions={0}, to_apply=%region_8.12 | sort | flops 106496 | bytes 131072 | tf_op jit(solution)/shard_map/jit(argsort)/sort | solution.py:34
  321.3 6.1 %gather_fusion.6 = s32[1024]{0:T(1024)S(1)} fusion(s32[8192]{0:T(1024)S(1)} %bitcast.115, s32[1024]{0:T(1024)S(1)} %fusion.80), kind=kCustom, calls=%fused_computation.8 | custom fusion | bytes 12288 | tf_op jit(solution)/shard_map/gather | solution.py:35
  327.4 6.8 %sort.94 = (s32[8192]{0:T(1024)}, s32[8192]{0:T(1024)S(1)}) sort(s32[8192]{0:T(1024)S(1)} %get-tuple-element.55, s32[8192]{0:T(1024)S(1)} %iota.143), dimensions={0}, to_apply=%region_7.11 | sort | flops 106496 | bytes 131072 | tf_op jit(solution)/shard_map/jit(argsort)/sort | solution.py:34
  337.4 6.8 %sort.92 = (s32[8192]{0:T(1024)}, s32[8192]{0:T(1024)S(1)}) sort(s32[8192]{0:T(1024)S(1)} %get-tuple-element.58, s32[8192]{0:T(1024)S(1)} %iota.138), dimensions={0}, to_apply=%region_4.7 | sort | flops 106496 | bytes 131072 | tf_op jit(solution)/shard_map/jit(argsort)/sort | solution.py:34
  347.5 6.8 %sort.93 = (s32[8192]{0:T(1024)}, s32[8192]{0:T(1024)S(1)}) sort(s32[8192]{0:T(1024)S(1)} %get-tuple-element.59, s32[8192]{0:T(1024)S(1)} %iota.140), dimensions={0}, to_apply=%region_5.8 | sort | flops 106496 | bytes 131072 | tf_op jit(solution)/shard_map/jit(argsort)/sort | solution.py:34
  354.3 6.1 %gather_fusion.4 = s32[1024]{0:T(1024)S(1)} fusion(s32[8192]{0:T(1024)S(1)} %bitcast.113, s32[1024]{0:T(1024)S(1)} %fusion.79), kind=kCustom, calls=%fused_computation.6 | custom fusion | bytes 12288 | tf_op jit(solution)/shard_map/gather | solution.py:35
  386.8 8.6 %gather_fusion.7 = f32[1536,768]{1,0:T(8,128)} fusion(f32[1025,768]{1,0:T(8,128)} %pad.15, s32[2048]{0:T(1024)S(1)} %pad_clamp_fusion.1), kind=kCustom, calls=%fused_computation.clone | custom fusion | bytes 9443328 | tf_op jit(solution)/shard_map/jit(_take)/gather | solution.py:171
  395.4 5.5 %gather_fusion.8 = f32[1536,768]{1,0:T(8,128)} fusion(f32[1025,768]{1,0:T(8,128)S(1)} %pad.16, s32[2048]{0:T(1024)S(1)} %pad_clamp_fusion), kind=kCustom, calls=%fused_computation.1.clone | custom fusion | bytes 9443328 | tf_op jit(solution)/shard_map/jit(_take)/gather | solution.py:171
  400.9 8.0 %select_add_fusion = f32[1536,768]{1,0:T(8,128)} fusion(f32[1536,768]{1,0:T(8,128)} %gather_fusion.8, f32[1536,768]{1,0:T(8,128)} %param.10, f32[1536,768]{1,0:T(8,128)} %gather_fusion.7, pred[1536]{0:T(1024)(128)(4,1)S(1)} %compare_and_fusion, pred[1536]{0:T(1024)(128)(4,1)S(1)} %compare_and_fusion.1), kind=kLoop, calls=%fused_computation.11 | loop fusion | flops 4718592 | bytes 18877440 | tf_op jit(solution)/shard_map/add | solution.py:171
  (205 shorter events, 101.9 us)
Async XLA Ops:
  7.2 84.2 %all-gather.4.cloned.1.call-start = ((), (), s32[]{:S(2)}) async-start(), calls=%async_computation.1 | async-start | bytes 2359296 | tf_op jit(solution)/shard_map/all_gather | solution.py:112
  8.8 9.7 %collective-permute-start.6 = (f32[128,512]{1,0:T(8,128)S(1)}, f32[128,512]{1,0:T(8,128)S(1)}, u32[]{:S(2)}, u32[]{:S(2)}) collective-permute-start(f32[128,512]{1,0:T(8,128)S(1)} %get-tuple-element.29), channel_id=1, source_target_pairs={{0,1},{8,9},{16,17},{24,25},{32,33},{40,41},{48,49},{56,57},{64,65... | collective-permute-start | bytes 786440 | tf_op jit(solution)/shard_map/ppermute | solution.py:106
  13.2 6.6 %collective-permute-start.5 = (f32[128,512]{1,0:T(8,128)S(1)}, f32[128,512]{1,0:T(8,128)S(1)}, u32[]{:S(2)}, u32[]{:S(2)}) collective-permute-start(f32[128,512]{1,0:T(8,128)S(1)} %get-tuple-element.30), channel_id=1, source_target_pairs={{0,2},{8,10},{16,18},{24,26},{32,34},{40,42},{48,50},{56,58},{64,6... | collective-permute-start | bytes 786440 | tf_op jit(solution)/shard_map/ppermute | solution.py:106
  14.5 10.6 %collective-permute-start.4 = (f32[128,512]{1,0:T(8,128)S(1)}, f32[128,512]{1,0:T(8,128)S(1)}, u32[]{:S(2)}, u32[]{:S(2)}) collective-permute-start(f32[128,512]{1,0:T(8,128)S(1)} %get-tuple-element.31), channel_id=1, source_target_pairs={{0,3},{8,11},{16,19},{24,27},{32,35},{40,43},{48,51},{56,59},{64,6... | collective-permute-start | bytes 786440 | tf_op jit(solution)/shard_map/ppermute | solution.py:106
  15.8 14.9 %collective-permute-start.3 = (f32[128,512]{1,0:T(8,128)S(1)}, f32[128,512]{1,0:T(8,128)S(1)}, u32[]{:S(2)}, u32[]{:S(2)}) collective-permute-start(f32[128,512]{1,0:T(8,128)S(1)} %get-tuple-element.32), channel_id=1, source_target_pairs={{0,4},{8,12},{16,20},{24,28},{32,36},{40,44},{48,52},{56,60},{64,6... | collective-permute-start | bytes 786440 | tf_op jit(solution)/shard_map/ppermute | solution.py:106
  17.1 19.2 %collective-permute-start.2 = (f32[128,512]{1,0:T(8,128)S(1)}, f32[128,512]{1,0:T(8,128)S(1)}, u32[]{:S(2)}, u32[]{:S(2)}) collective-permute-start(f32[128,512]{1,0:T(8,128)S(1)} %get-tuple-element.33), channel_id=1, source_target_pairs={{0,5},{8,13},{16,21},{24,29},{32,37},{40,45},{48,53},{56,61},{64,6... | collective-permute-start | bytes 786440 | tf_op jit(solution)/shard_map/ppermute | solution.py:106
  18.5 17.8 %collective-permute-start.1 = (f32[128,512]{1,0:T(8,128)S(1)}, f32[128,512]{1,0:T(8,128)S(1)}, u32[]{:S(2)}, u32[]{:S(2)}) collective-permute-start(f32[128,512]{1,0:T(8,128)S(1)} %get-tuple-element.34), channel_id=1, source_target_pairs={{0,6},{8,14},{16,22},{24,30},{32,38},{40,46},{48,54},{56,62},{64,7... | collective-permute-start | bytes 786440 | tf_op jit(solution)/shard_map/ppermute | solution.py:106
  19.8 16.5 %collective-permute-start = (f32[128,512]{1,0:T(8,128)S(1)}, f32[128,512]{1,0:T(8,128)S(1)}, u32[]{:S(2)}, u32[]{:S(2)}) collective-permute-start(f32[128,512]{1,0:T(8,128)S(1)} %get-tuple-element.35), channel_id=1, source_target_pairs={{0,7},{8,15},{16,23},{24,31},{32,39},{40,47},{48,55},{56,63},{64,7... | collective-permute-start | bytes 786440 | tf_op jit(solution)/shard_map/ppermute | solution.py:106
  38.2 76.6 %copy-start.24 = (s32[2]{0:T(128)S(1)}, s32[2]{0:T(128)}, u32[]{:S(2)}) copy-start(s32[2]{0:T(128)} %param.12) | copy-start | bytes 28
  38.2 113.1 %all-gather.6.cloned.1.call-start = ((), (), s32[]{:S(2)}) async-start(), calls=%async_computation.2 | async-start | bytes 3538944 | tf_op jit(solution)/shard_map/all_gather | solution.py:124
  92.7 4.8 %collective-permute-start.14 = (f32[64,512]{1,0:T(8,128)S(1)}, f32[64,512]{1,0:T(8,128)S(1)}, u32[]{:S(2)}, u32[]{:S(2)}) collective-permute-start(f32[64,512]{1,0:T(8,128)S(1)} %get-tuple-element.36), channel_id=1, source_target_pairs={{0,8},{1,9},{2,10},{3,11},{4,12},{5,13},{6,14},{7,15},{64,72},{65,... | collective-permute-start | bytes 393224 | tf_op jit(solution)/shard_map/ppermute | solution.py:120
  94.0 4.2 %collective-permute-start.13 = (f32[64,512]{1,0:T(8,128)S(1)}, f32[64,512]{1,0:T(8,128)S(1)}, u32[]{:S(2)}, u32[]{:S(2)}) collective-permute-start(f32[64,512]{1,0:T(8,128)S(1)} %get-tuple-element.37), channel_id=1, source_target_pairs={{0,16},{1,17},{2,18},{3,19},{4,20},{5,21},{6,22},{7,23},{64,80},{6... | collective-permute-start | bytes 393224 | tf_op jit(solution)/shard_map/ppermute | solution.py:120
  94.7 5.2 %collective-permute-start.12 = (f32[64,512]{1,0:T(8,128)S(1)}, f32[64,512]{1,0:T(8,128)S(1)}, u32[]{:S(2)}, u32[]{:S(2)}) collective-permute-start(f32[64,512]{1,0:T(8,128)S(1)} %get-tuple-element.38), channel_id=1, source_target_pairs={{0,24},{1,25},{2,26},{3,27},{4,28},{5,29},{6,30},{7,31},{64,88},{6... | collective-permute-start | bytes 393224 | tf_op jit(solution)/shard_map/ppermute | solution.py:120
  95.3 14.7 %collective-permute-start.11 = (f32[64,512]{1,0:T(8,128)S(1)}, f32[64,512]{1,0:T(8,128)S(1)}, u32[]{:S(2)}, u32[]{:S(2)}) collective-permute-start(f32[64,512]{1,0:T(8,128)S(1)} %get-tuple-element.39), channel_id=1, source_target_pairs={{0,32},{1,33},{2,34},{3,35},{4,36},{5,37},{6,38},{7,39},{64,96},{6... | collective-permute-start | bytes 393224 | tf_op jit(solution)/shard_map/ppermute | solution.py:120
  96.0 14.0 %collective-permute-start.10 = (f32[64,512]{1,0:T(8,128)S(1)}, f32[64,512]{1,0:T(8,128)S(1)}, u32[]{:S(2)}, u32[]{:S(2)}) collective-permute-start(f32[64,512]{1,0:T(8,128)S(1)} %get-tuple-element.40), channel_id=1, source_target_pairs={{0,40},{1,41},{2,42},{3,43},{4,44},{5,45},{6,46},{7,47},{64,104},{... | collective-permute-start | bytes 393224 | tf_op jit(solution)/shard_map/ppermute | solution.py:120
  97.5 12.6 %collective-permute-start.9 = (f32[64,512]{1,0:T(8,128)S(1)}, f32[64,512]{1,0:T(8,128)S(1)}, u32[]{:S(2)}, u32[]{:S(2)}) collective-permute-start(f32[64,512]{1,0:T(8,128)S(1)} %get-tuple-element.41), channel_id=1, source_target_pairs={{0,48},{1,49},{2,50},{3,51},{4,52},{5,53},{6,54},{7,55},{64,112},{... | collective-permute-start | bytes 393224 | tf_op jit(solution)/shard_map/ppermute | solution.py:120
  98.2 11.9 %collective-permute-start.8 = (f32[64,512]{1,0:T(8,128)S(1)}, f32[64,512]{1,0:T(8,128)S(1)}, u32[]{:S(2)}, u32[]{:S(2)}) collective-permute-start(f32[64,512]{1,0:T(8,128)S(1)} %get-tuple-element.42), channel_id=1, source_target_pairs={{0,56},{1,57},{2,58},{3,59},{4,60},{5,61},{6,62},{7,63},{64,120},{... | collective-permute-start | bytes 393224 | tf_op jit(solution)/shard_map/ppermute | solution.py:120
  99.8 14.2 %collective-permute-start.7 = (f32[128,512]{1,0:T(8,128)S(1)}, f32[128,512]{1,0:T(8,128)S(1)}, u32[]{:S(2)}, u32[]{:S(2)}) collective-permute-start(f32[128,512]{1,0:T(8,128)S(1)} %constant_dynamic-slice_fusion), channel_id=1, source_target_pairs={{0,0},{1,8},{2,16},{3,24},{4,32},{5,40},{6,48},{7,56},{8,1},{9,9},... | collective-permute-start | bytes 786440 | tf_op jit(solution)/shard_map/ppermute | solution.py:116
  234.3 30.2 %copy-start.3 = (f32[8,128,512]{2,1,0:T(8,128)S(1)}, f32[8,128,512]{2,1,0:T(8,128)}, u32[]{:S(2)}) copy-start(f32[8,128,512]{2,1,0:T(8,128)} %slice.219) | copy-start | bytes 6291460
  261.3 9.2 %copy-start.19 = (f32[128,128]{1,0:T(8,128)}, f32[128,128]{1,0:T(8,128)S(1)}, u32[]{:S(2)}) copy-start(f32[128,128]{1,0:T(8,128)S(1)} %copy.51) | copy-start | bytes 196612
  261.9 8.6 %copy-start.14 = (f32[128,128]{1,0:T(8,128)}, f32[128,128]{1,0:T(8,128)S(1)}, u32[]{:S(2)}) copy-start(f32[128,128]{1,0:T(8,128)S(1)} %convolution_negate_fusion.2) | copy-start | bytes 196612
  262.2 8.3 %copy-start.15 = (f32[128,128]{1,0:T(8,128)}, f32[128,128]{1,0:T(8,128)S(1)}, u32[]{:S(2)}) copy-start(f32[128,128]{1,0:T(8,128)S(1)} %convolution_negate_fusion) | copy-start | bytes 196612
  263.1 7.5 %copy-start.16 = (f32[128,128]{1,0:T(8,128)}, f32[128,128]{1,0:T(8,128)S(1)}, u32[]{:S(2)}) copy-start(f32[128,128]{1,0:T(8,128)S(1)} %convolution_negate_fusion.1) | copy-start | bytes 196612
  264.6 6.1 %copy-start.4 = (f32[1024,512]{1,0:T(8,128)S(1)}, f32[1024,512]{1,0:T(8,128)}, u32[]{:S(2)}) copy-start(f32[1024,512]{1,0:T(8,128)} %all-gather.4.cloned.1.call-done) | copy-start | bytes 6291460
  264.6 6.1 %copy-start.17 = (f32[128,128]{1,0:T(8,128)S(1)}, f32[128,128]{1,0:T(8,128)}, u32[]{:S(2)}) copy-start(f32[128,128]{1,0:T(8,128)} %copy.44) | copy-start | bytes 196612
  264.6 6.1 %copy-start.18 = (f32[128,128]{1,0:T(8,128)S(1)}, f32[128,128]{1,0:T(8,128)}, u32[]{:S(2)}) copy-start(f32[128,128]{1,0:T(8,128)} %copy.47) | copy-start | bytes 196612
  264.7 6.1 %copy-start.20 = (pred[1024]{0:T(1024)(128)(4,1)S(1)}, pred[1024]{0:T(1024)(128)(4,1)}, u32[]{:S(2)}) copy-start(pred[1024]{0:T(1024)(128)(4,1)} %get-tuple-element.60) | copy-start | bytes 3076
  280.6 9.9 %copy-start.2 = (f32[1024,1024]{1,0:T(8,128)S(1)}, f32[1024,1024]{1,0:T(8,128)}, u32[]{:S(2)}) copy-start(f32[1024,1024]{1,0:T(8,128)} %gather_fusion.1) | copy-start | bytes 12582916
  280.6 9.9 %copy-start.22 = (pred[1024]{0:T(1024)(128)(4,1)S(1)}, pred[1024]{0:T(1024)(128)(4,1)}, u32[]{:S(2)}) copy-start(pred[1024]{0:T(1024)(128)(4,1)} %fusion.92) | copy-start | bytes 3076
  280.6 9.9 %copy-start.23 = (s32[1024]{0:T(1024)S(1)}, s32[1024]{0:T(1024)}, u32[]{:S(2)}) copy-start(s32[1024]{0:T(1024)} %get-tuple-element.11) | copy-start | bytes 12292
  303.4 10.9 %copy-start.13 = (s32[2,8192]{1,0:T(2,128)S(1)}, s32[2,8192]{1,0:T(2,128)}, u32[]{:S(2)}) copy-start(s32[2,8192]{1,0:T(2,128)} %param.11) | copy-start | bytes 196612
  303.4 65.9 %all-to-all-start = ((f32[128,64,128]{2,1,0:T(8,128)}), f32[128,64,128]{2,1,0:T(8,128)}, u32[]{:S(2)}, u32[]{:S(2)}) async-start(f32[128,64,128]{2,1,0:T(8,128)} %bitcast.121), calls=%async_computation | async-start | bytes 8388608 | tf_op jit(solution)/shard_map/all_to_all | solution.py:153
  (11 other events, 60.6 us)
Sparse Core Ops, SparseCore 0:
  38.3 52.9 all-gather.3
  115.0 36.3 all-gather.5
where the time goes:
time: 420 us; the launch traced here: 416 us
  other arithmetic  147 us (35%)
  local copies, waits for them, and re-layouts  93 us (22%)
  waiting for transfers between devices  78.2 us (19%)
  matrix products  43.5 us (10%)
  starting transfers between devices  38.7 us (9%)
  between operations  15.8 us (4%)
    all_gather x1, waiting for transfers between devices, on_device(): columns = lax.all_gather(first_piece, 'col', axis=0, tiled=True)  53.1 us
    another operation x12, other arithmetic, factor_and_invert(): factor[k, k] = jnp.linalg.cholesky(trailing[:size, :size])  50.4 us
    another operation x8, other arithmetic, factor_and_invert(): lax.linalg.triangular_solve(factor[k, k], eye, left_side=True, lower=True)  43.2 us
    sort x4, other arithmetic, select_rows(): chosen = jnp.argsort(keyed)[:count]  27 us
    gather x4, local copies, waits for them, and re-layouts, select_rows(): return parent_map[chosen] - owner * width  18.8 us
    ppermute x7, waiting for transfers between devices, on_device(): lax.ppermute(block_here[target * panel_rows:(target + 1) * panel_rows, :P...  15.2 us
    gather x2, local copies, waits for them, and re-layouts, on_device(): assembled = assembled + jnp.take(padded, row_lookup, axis=0)  14.1 us
    ppermute x7, starting transfers between devices, on_device(): lax.ppermute(block_here[target * panel_rows:(target + 1) * panel_rows, :P...  12.2 us
  transfers between devices with their start and end apart: 18, of which 7 were waited for; matrix products, arithmetic and copies ran while one was open for 21% of the time, Pallas kernels for 0%

commit v1 on v0

--- a/solution.py
+++ b/solution.py
@@ -109,7 +109,9 @@
             [(0, target)],
         )
         first_piece = jnp.where(col_index == target, moved, first_piece)
-    columns = lax.all_gather(first_piece, "col", axis=0, tiled=True)
+    columns = jnp.concatenate(
+        lax.all_to_all(jnp.stack([first_piece] * lax.axis_size("col")), "col", 0, 0), axis=0
+    )
     part_rows = rows_here // n_row
     own_piece = lax.dynamic_slice_in_dim(columns, col_index * part_rows, part_rows)
     pairs = [(n_col * a + b, n_col * b + a) for a in range(n_row) for b in range(n_col)]

time: 420 us -> 397 us (0.945)
  waiting for transfers between devices: 78.2 us -> 24.3 us
  blocking collectives: 0 us -> 30.2 us
    all_gather x1 -> x0, waiting for transfers between devices: 53.1 us -> none  [on_device(): columns = lax.all_gather(first_piece, 'col', axis=0, tiled=True)]
    all_to_all x0 -> x1, blocking collectives: none -> 30.2 us  [on_device(): lax.all_to_all(jnp.stack([first_piece] * lax.axis_size('col')), 'col', 0, 0)]
  transfers between devices with their start and end apart: 18 -> 17, of which waited for: 7 -> 5; matrix products, arithmetic and copies ran while one was open for 21% -> 22% of each run, Pallas kernels for 0% -> 0%
where the time goes in v1:
time: 397 us; the launch traced here: 392 us
  other arithmetic  145 us (37%)
  local copies, waits for them, and re-layouts  91 us (23%)
  matrix products  43.5 us (11%)
  starting transfers between devices  42.3 us (11%)
  blocking collectives  30.2 us (8%)
  waiting for transfers between devices  24.3 us (6%)
  between operations  15.8 us (4%)
    another operation x12, other arithmetic, factor_and_invert(): factor[k, k] = jnp.linalg.cholesky(trailing[:size, :size])  50.4 us
    another operation x8, other arithmetic, factor_and_invert(): lax.linalg.triangular_solve(factor[k, k], eye, left_side=True, lower=True)  43.2 us
    all_to_all x1, blocking collectives, on_device(): lax.all_to_all(jnp.stack([first_piece] * lax.axis_size('col')), 'col', 0, 0)  30.2 us
    sort x4, other arithmetic, select_rows(): chosen = jnp.argsort(keyed)[:count]  27 us
    gather x4, local copies, waits for them, and re-layouts, select_rows(): return parent_map[chosen] - owner * width  18.8 us
    ppermute x7, waiting for transfers between devices, on_device(): lax.ppermute(block_here[target * panel_rows:(target + 1) * panel_rows, :P...  15.2 us
    gather x2, local copies, waits for them, and re-layouts, on_device(): assembled = assembled + jnp.take(padded, row_lookup, axis=0)  14.1 us
    ppermute x7, starting transfers between devices, on_device(): lax.ppermute(block_here[target * panel_rows:(target + 1) * panel_rows, :P...  12.2 us
  transfers between devices with their start and end apart: 17, of which 5 were waited for; matrix products, arithmetic and copies ran while one was open for 22% of the time, Pallas kernels for 0%

profile of v1, /device:TPU:1, one launch (start us, length us, event | category | flops | bytes accessed | tf_op | source)
XLA Modules:
  0.0 392.4 jit_solution(5180303394732462482)
XLA Ops:
  8.8 4.4 %collective-permute-start.6 = (f32[128,512]{1,0:T(8,128)S(1)}, f32[128,512]{1,0:T(8,128)S(1)}, u32[]{:S(2)}, u32[]{:S(2)}) collective-permute-start(f32[128,512]{1,0:T(8,128)S(1)} %get-tuple-element.29), channel_id=1, source_target_pairs={{0,1},{8,9},{16,17},{24,25},{32,33},{40,41},{48,49},{56,57},{64,65... | collective-permute-start | bytes 786440 | tf_op jit(solution)/shard_map/ppermute | solution.py:106
  25.1 5.6 %collective-permute-done.3 = f32[128,512]{1,0:T(8,128)S(1)} collective-permute-done((f32[128,512]{1,0:T(8,128)S(1)}, f32[128,512]{1,0:T(8,128)S(1)}, u32[]{:S(2)}, u32[]{:S(2)}) %collective-permute-start.3) | collective-permute-done | bytes 262176 | tf_op jit(solution)/shard_map/ppermute | solution.py:106
  30.7 5.6 %collective-permute-done.2 = f32[128,512]{1,0:T(8,128)S(1)} collective-permute-done((f32[128,512]{1,0:T(8,128)S(1)}, f32[128,512]{1,0:T(8,128)S(1)}, u32[]{:S(2)}, u32[]{:S(2)}) %collective-permute-start.2) | collective-permute-done | bytes 262176 | tf_op jit(solution)/shard_map/ppermute | solution.py:106
  37.8 30.2 %all_to_all.14 = f32[8,128,512]{2,1,0:T(8,128)S(1)} all-to-all(f32[8,128,512]{2,1,0:T(8,128)S(1)} %stack.2), channel_id=1, replica_groups=mesh['child'=2,'row'=8,'col'=8] {'col'}, dimensions={0} | all-to-all | bytes 4194304 | tf_op jit(solution)/shard_map/all_to_all | solution.py:113
  76.0 11.4 %collective-permute-start.7 = (f32[128,512]{1,0:T(8,128)S(1)}, f32[128,512]{1,0:T(8,128)S(1)}, u32[]{:S(2)}, u32[]{:S(2)}) collective-permute-start(f32[128,512]{1,0:T(8,128)S(1)} %constant_dynamic-slice_fusion), channel_id=1, source_target_pairs={{0,0},{1,8},{2,16},{3,24},{4,32},{5,40},{6,48},{7,56},{8,1},{9,9},... | collective-permute-start | bytes 786440 | tf_op jit(solution)/shard_map/ppermute | solution.py:118
  99.1 8.5 %gather_fusion.1 = f32[1024,1024]{1,0:T(8,128)} fusion(f32[1024,1024]{1,0:T(8,128)} %bitcast.120, s32[1024]{0:T(1024)S(1)} %fusion.78), kind=kCustom, calls=%fused_computation.3 | custom fusion | bytes 8392704 | tf_op jit(solution)/shard_map/gather | solution.py:144
  108.2 7.0 %gather_fusion = pred[1024]{0:T(1024)(128)(4,1)S(1)} fusion(pred[1024]{0:T(1024)(128)(4,1)S(1)} %fusion.91, s32[1024]{0:T(1024)S(1)} %fusion.78), kind=kCustom, calls=%fused_computation.2 | custom fusion | bytes 6144 | tf_op jit(solution)/shard_map/gather | solution.py:147
  115.2 4.4 %sort.90 = (s32[1024]{0:T(1024)}, s32[1024]{0:T(1024)}) sort(s32[1024]{0:T(1024)S(1)} %get-tuple-element.62, s32[1024]{0:T(1024)S(1)} %iota.129), dimensions={0}, to_apply=%region_0.1 | sort | flops 10240 | bytes 16384 | tf_op jit(solution)/shard_map/jit(argsort)/sort | solution.py:139
  122.5 5.2 %all-gather.3.cloned.1.call-done = f32[1536,512]{1,0:T(8,128)} async-done(((f32[192,512]{1,0:T(8,128)}), f32[1536,512]{1,0:T(8,128)}) %all-gather.3.cloned.1.call-update) | async-done | bytes 3145744 | tf_op jit(solution)/shard_map/all_gather | solution.py:126
  132.9 11.7 %cholesky.74 = f32[128,128]{1,0:T(8,128)S(1)} custom-call(f32[128,128]{1,0:T(8,128)S(1)} %fusion.64), custom_call_target="Cholesky" | custom-call | tf_op jit(solution)/shard_map/jit(cholesky)/cholesky | solution.py:60
  146.1 9.8 %custom-call.8 = f32[1,128,128]{1,2,0:T(8,128)S(1)} custom-call(f32[1,128,128]{2,1,0:T(8,128)S(1)} %get-tuple-element.25), custom_call_target="InvertDiagBlocksLowerTriangular" | custom-call | tf_op jit(solution)/shard_map/triangular_solve/custom-call.0 | solution.py:61
  158.2 12.1 %cholesky.85 = f32[128,128]{1,0:T(8,128)S(1)} custom-call(f32[128,128]{1,0:T(8,128)S(1)} %fusion.62), custom_call_target="Cholesky" | custom-call | tf_op jit(solution)/shard_map/jit(cholesky)/cholesky | solution.py:60
  172.4 9.8 %custom-call.9 = f32[1,128,128]{1,2,0:T(8,128)S(1)} custom-call(f32[1,128,128]{2,1,0:T(8,128)S(1)} %get-tuple-element.23), custom_call_target="InvertDiagBlocksLowerTriangular" | custom-call | tf_op jit(solution)/shard_map/triangular_solve/custom-call.0 | solution.py:61
  184.1 11.7 %cholesky.96 = f32[128,128]{1,0:T(8,128)S(1)} custom-call(f32[128,128]{1,0:T(8,128)S(1)} %fusion.60), custom_call_target="Cholesky" | custom-call | tf_op jit(solution)/shard_map/jit(cholesky)/cholesky | solution.py:60
  197.7 9.8 %custom-call.10 = f32[1,128,128]{1,2,0:T(8,128)S(1)} custom-call(f32[1,128,128]{2,1,0:T(8,128)S(1)} %get-tuple-element.21), custom_call_target="InvertDiagBlocksLowerTriangular" | custom-call | tf_op jit(solution)/shard_map/triangular_solve/custom-call.0 | solution.py:61
  214.2 11.9 %cholesky.107 = f32[128,128]{1,0:T(8,128)S(1)} custom-call(f32[128,128]{1,0:T(8,128)S(1)} %fusion.58), custom_call_target="Cholesky" | custom-call | tf_op jit(solution)/shard_map/jit(cholesky)/cholesky | solution.py:60
  227.5 9.8 %custom-call.11 = f32[1,128,128]{1,2,0:T(8,128)S(1)} custom-call(f32[1,128,128]{2,1,0:T(8,128)S(1)} %get-tuple-element.19), custom_call_target="InvertDiagBlocksLowerTriangular" | custom-call | tf_op jit(solution)/shard_map/triangular_solve/custom-call.0 | solution.py:61
  241.1 5.8 %fusion.107 = f32[1024,512]{1,0:T(8,128)} fusion(f32[1024,512]{1,0:T(8,128)S(1)} %bitcast.135, f32[128,256]{1,0:T(8,128)S(1)} %broadcast.201, f32[128,128]{1,0:T(8,128)S(1)} %cholesky.75, f32[128,128]{1,0:T(8,128)S(1)} %fusion.45, f32[128,128]{1,0:T(8,128)S(1)} %copy.51, f32[128,128]{1,0:T(8,128)S(1)} %convolution_negate_fusion, ...), kind=kOutput, calls=%fused_computation.207 | convolution fusion | flops 3224633344 | bytes 5046272 | tf_op jit(solution)/shard_map/dot_general | solution.py:85
  247.2 4.9 %fusion.8 = f32[1024,512]{1,0:T(8,128)S(1)} fusion(f32[512,512]{1,0:T(8,128)S(1)} %fusion.21, f32[1024,512]{1,0:T(8,128)S(1)} %bitcast.132, pred[1024]{0:T(1024)(128)(4,1)S(1)} %copy-done.21, pred[1024]{0:T(1024)(128)(4,1)S(1)} %copy-done.22, f32[128,256]{1,0:T(8,128)S(1)} %broadcast.201, f32[128,128]{1,0:T(8,128)S(1)} %cholesky.75, ...), kind=kOutput, calls=%fused_computation.22 | convolution fusion | flops 3225681920 | bytes 6096896 | tf_op jit(solution)/shard_map/dot_general | solution.py:85
  252.1 4.9 %gather_fusion.2 = f32[1024,512]{1,0:T(8,128)} fusion(f32[1024,512]{1,0:T(8,128)S(1)} %fusion.8, s32[1024]{0:T(1024)S(1)} %fusion.78), kind=kCustom, calls=%fused_computation.4 | custom fusion | bytes 4198400 | tf_op jit(solution)/shard_map/gather | solution.py:145
  257.0 9.8 %fusion.10 = f32[1024,1024]{1,0:T(8,128)S(1)} fusion(f32[1024,512]{1,0:T(8,128)} %gather_fusion.2, f32[1024,512]{1,0:T(8,128)} %fusion.107, f32[512,512]{1,0:T(8,128)S(1)} %fusion.21, pred[1024]{0:T(1024)(128)(4,1)S(1)} %get-tuple-element.56, pred[1024]{0:T(1024)(128)(4,1)S(1)} %get-tuple-element.57), kind=kOutput, calls=%fused_computation.24 | convolution fusion | flops 6443499520 | bytes 9439232 | tf_op jit(solution)/shard_map/dot_general | solution.py:144
  266.9 9.0 %fusion.5 = f32[128,8,8,128]{3,1,2,0:T(8,128)S(1)} fusion(f32[1024,1024]{1,0:T(8,128)S(1)} %copy-done.4, f32[1024,1024]{1,0:T(8,128)S(1)} %fusion.10, s32[1024]{0:T(1024)S(1)} %copy-done.24, pred[1024]{0:T(1024)(128)(4,1)S(1)} %copy-done.23, pred[1024]{0:T(1024)(128)(4,1)S(1)} %gather_fusion), kind=kOutput, calls=%fused_computation.21 | convolution fusion | flops 12890144768 | bytes 12589056 | tf_op jit(solution)/shard_map/qj,iq->ji/dot_general | solution.py:148
  279.8 10.7 %all-to-all-start.1 = ((f32[128,64,128]{2,1,0:T(8,128)}), f32[128,64,128]{2,1,0:T(8,128)}, u32[]{:S(2)}, u32[]{:S(2)}) async-start(f32[128,64,128]{2,1,0:T(8,128)} %bitcast.122), calls=%async_computation.1 | async-start | bytes 8388608 | tf_op jit(solution)/shard_map/all_to_all | solution.py:155
  290.7 6.8 %sort.95 = (s32[8192]{0:T(1024)}, s32[8192]{0:T(1024)S(1)}) sort(s32[8192]{0:T(1024)S(1)} %get-tuple-element.54, s32[8192]{0:T(1024)S(1)} %iota.145), dimensions={0}, to_apply=%region_8.12 | sort | flops 106496 | bytes 131072 | tf_op jit(solution)/shard_map/jit(argsort)/sort | solution.py:34
  297.5 6.1 %gather_fusion.6 = s32[1024]{0:T(1024)S(1)} fusion(s32[8192]{0:T(1024)S(1)} %bitcast.116, s32[1024]{0:T(1024)S(1)} %fusion.80), kind=kCustom, calls=%fused_computation.8 | custom fusion | bytes 12288 | tf_op jit(solution)/shard_map/gather | solution.py:35
  303.6 6.8 %sort.94 = (s32[8192]{0:T(1024)}, s32[8192]{0:T(1024)S(1)}) sort(s32[8192]{0:T(1024)S(1)} %get-tuple-element.55, s32[8192]{0:T(1024)S(1)} %iota.143), dimensions={0}, to_apply=%region_7.11 | sort | flops 106496 | bytes 131072 | tf_op jit(solution)/shard_map/jit(argsort)/sort | solution.py:34
  313.6 6.8 %sort.92 = (s32[8192]{0:T(1024)}, s32[8192]{0:T(1024)S(1)}) sort(s32[8192]{0:T(1024)S(1)} %get-tuple-element.58, s32[8192]{0:T(1024)S(1)} %iota.138), dimensions={0}, to_apply=%region_4.7 | sort | flops 106496 | bytes 131072 | tf_op jit(solution)/shard_map/jit(argsort)/sort | solution.py:34
  323.7 6.8 %sort.93 = (s32[8192]{0:T(1024)}, s32[8192]{0:T(1024)S(1)}) sort(s32[8192]{0:T(1024)S(1)} %get-tuple-element.59, s32[8192]{0:T(1024)S(1)} %iota.140), dimensions={0}, to_apply=%region_5.8 | sort | flops 106496 | bytes 131072 | tf_op jit(solution)/shard_map/jit(argsort)/sort | solution.py:34
  330.5 6.1 %gather_fusion.4 = s32[1024]{0:T(1024)S(1)} fusion(s32[8192]{0:T(1024)S(1)} %bitcast.114, s32[1024]{0:T(1024)S(1)} %fusion.79), kind=kCustom, calls=%fused_computation.6 | custom fusion | bytes 12288 | tf_op jit(solution)/shard_map/gather | solution.py:35
  363.0 8.6 %gather_fusion.7 = f32[1536,768]{1,0:T(8,128)} fusion(f32[1025,768]{1,0:T(8,128)} %pad.15, s32[2048]{0:T(1024)S(1)} %pad_clamp_fusion.1), kind=kCustom, calls=%fused_computation.clone | custom fusion | bytes 9443328 | tf_op jit(solution)/shard_map/jit(_take)/gather | solution.py:173
  371.6 5.5 %gather_fusion.8 = f32[1536,768]{1,0:T(8,128)} fusion(f32[1025,768]{1,0:T(8,128)S(1)} %pad.16, s32[2048]{0:T(1024)S(1)} %pad_clamp_fusion), kind=kCustom, calls=%fused_computation.1.clone | custom fusion | bytes 9443328 | tf_op jit(solution)/shard_map/jit(_take)/gather | solution.py:173
  377.1 8.0 %select_add_fusion = f32[1536,768]{1,0:T(8,128)} fusion(f32[1536,768]{1,0:T(8,128)} %gather_fusion.8, f32[1536,768]{1,0:T(8,128)} %param.10, f32[1536,768]{1,0:T(8,128)} %gather_fusion.7, pred[1536]{0:T(1024)(128)(4,1)S(1)} %compare_and_fusion, pred[1536]{0:T(1024)(128)(4,1)S(1)} %compare_and_fusion.1), kind=kLoop, calls=%fused_computation.11 | loop fusion | flops 4718592 | bytes 18877440 | tf_op jit(solution)/shard_map/add | solution.py:173
  (206 shorter events, 100.8 us)
Async XLA Ops:
  7.2 120.5 %all-gather.3.cloned.1.call-start = ((), (), s32[]{:S(2)}) async-start(), calls=%async_computation.2 | async-start | bytes 3538944 | tf_op jit(solution)/shard_map/all_gather | solution.py:126
  8.8 9.7 %collective-permute-start.6 = (f32[128,512]{1,0:T(8,128)S(1)}, f32[128,512]{1,0:T(8,128)S(1)}, u32[]{:S(2)}, u32[]{:S(2)}) collective-permute-start(f32[128,512]{1,0:T(8,128)S(1)} %get-tuple-element.29), channel_id=1, source_target_pairs={{0,1},{8,9},{16,17},{24,25},{32,33},{40,41},{48,49},{56,57},{64,65... | collective-permute-start | bytes 786440 | tf_op jit(solution)/shard_map/ppermute | solution.py:106
  13.2 6.6 %collective-permute-start.5 = (f32[128,512]{1,0:T(8,128)S(1)}, f32[128,512]{1,0:T(8,128)S(1)}, u32[]{:S(2)}, u32[]{:S(2)}) collective-permute-start(f32[128,512]{1,0:T(8,128)S(1)} %get-tuple-element.30), channel_id=1, source_target_pairs={{0,2},{8,10},{16,18},{24,26},{32,34},{40,42},{48,50},{56,58},{64,6... | collective-permute-start | bytes 786440 | tf_op jit(solution)/shard_map/ppermute | solution.py:106
  14.5 10.6 %collective-permute-start.4 = (f32[128,512]{1,0:T(8,128)S(1)}, f32[128,512]{1,0:T(8,128)S(1)}, u32[]{:S(2)}, u32[]{:S(2)}) collective-permute-start(f32[128,512]{1,0:T(8,128)S(1)} %get-tuple-element.31), channel_id=1, source_target_pairs={{0,3},{8,11},{16,19},{24,27},{32,35},{40,43},{48,51},{56,59},{64,6... | collective-permute-start | bytes 786440 | tf_op jit(solution)/shard_map/ppermute | solution.py:106
  15.8 14.9 %collective-permute-start.3 = (f32[128,512]{1,0:T(8,128)S(1)}, f32[128,512]{1,0:T(8,128)S(1)}, u32[]{:S(2)}, u32[]{:S(2)}) collective-permute-start(f32[128,512]{1,0:T(8,128)S(1)} %get-tuple-element.32), channel_id=1, source_target_pairs={{0,4},{8,12},{16,20},{24,28},{32,36},{40,44},{48,52},{56,60},{64,6... | collective-permute-start | bytes 786440 | tf_op jit(solution)/shard_map/ppermute | solution.py:106
  17.1 19.2 %collective-permute-start.2 = (f32[128,512]{1,0:T(8,128)S(1)}, f32[128,512]{1,0:T(8,128)S(1)}, u32[]{:S(2)}, u32[]{:S(2)}) collective-permute-start(f32[128,512]{1,0:T(8,128)S(1)} %get-tuple-element.33), channel_id=1, source_target_pairs={{0,5},{8,13},{16,21},{24,29},{32,37},{40,45},{48,53},{56,61},{64,6... | collective-permute-start | bytes 786440 | tf_op jit(solution)/shard_map/ppermute | solution.py:106
  18.5 17.8 %collective-permute-start.1 = (f32[128,512]{1,0:T(8,128)S(1)}, f32[128,512]{1,0:T(8,128)S(1)}, u32[]{:S(2)}, u32[]{:S(2)}) collective-permute-start(f32[128,512]{1,0:T(8,128)S(1)} %get-tuple-element.34), channel_id=1, source_target_pairs={{0,6},{8,14},{16,22},{24,30},{32,38},{40,46},{48,54},{56,62},{64,7... | collective-permute-start | bytes 786440 | tf_op jit(solution)/shard_map/ppermute | solution.py:106
  19.8 16.5 %collective-permute-start = (f32[128,512]{1,0:T(8,128)S(1)}, f32[128,512]{1,0:T(8,128)S(1)}, u32[]{:S(2)}, u32[]{:S(2)}) collective-permute-start(f32[128,512]{1,0:T(8,128)S(1)} %get-tuple-element.35), channel_id=1, source_target_pairs={{0,7},{8,15},{16,23},{24,31},{32,39},{40,47},{48,55},{56,63},{64,7... | collective-permute-start | bytes 786440 | tf_op jit(solution)/shard_map/ppermute | solution.py:106
  68.0 24.3 %copy-start.2 = (f32[8,128,512]{2,1,0:T(8,128)}, f32[8,128,512]{2,1,0:T(8,128)S(1)}, u32[]{:S(2)}) copy-start(f32[8,128,512]{2,1,0:T(8,128)S(1)} %all_to_all.14) | copy-start | bytes 6291460
  68.0 24.3 %copy-start.25 = (s32[2]{0:T(128)S(1)}, s32[2]{0:T(128)}, u32[]{:S(2)}) copy-start(s32[2]{0:T(128)} %param.12) | copy-start | bytes 28
  68.1 5.3 %collective-permute-start.14 = (f32[64,512]{1,0:T(8,128)S(1)}, f32[64,512]{1,0:T(8,128)S(1)}, u32[]{:S(2)}, u32[]{:S(2)}) collective-permute-start(f32[64,512]{1,0:T(8,128)S(1)} %get-tuple-element.36), channel_id=1, source_target_pairs={{0,8},{1,9},{2,10},{3,11},{4,12},{5,13},{6,14},{7,15},{64,72},{65,... | collective-permute-start | bytes 393224 | tf_op jit(solution)/shard_map/ppermute | solution.py:122
  69.4 5.3 %collective-permute-start.13 = (f32[64,512]{1,0:T(8,128)S(1)}, f32[64,512]{1,0:T(8,128)S(1)}, u32[]{:S(2)}, u32[]{:S(2)}) collective-permute-start(f32[64,512]{1,0:T(8,128)S(1)} %get-tuple-element.37), channel_id=1, source_target_pairs={{0,16},{1,17},{2,18},{3,19},{4,20},{5,21},{6,22},{7,23},{64,80},{6... | collective-permute-start | bytes 393224 | tf_op jit(solution)/shard_map/ppermute | solution.py:122
  70.0 5.9 %collective-permute-start.12 = (f32[64,512]{1,0:T(8,128)S(1)}, f32[64,512]{1,0:T(8,128)S(1)}, u32[]{:S(2)}, u32[]{:S(2)}) collective-permute-start(f32[64,512]{1,0:T(8,128)S(1)} %get-tuple-element.38), channel_id=1, source_target_pairs={{0,24},{1,25},{2,26},{3,27},{4,28},{5,29},{6,30},{7,31},{64,88},{6... | collective-permute-start | bytes 393224 | tf_op jit(solution)/shard_map/ppermute | solution.py:122
  70.7 16.7 %collective-permute-start.11 = (f32[64,512]{1,0:T(8,128)S(1)}, f32[64,512]{1,0:T(8,128)}, u32[]{:S(2)}, u32[]{:S(2)}) collective-permute-start(f32[64,512]{1,0:T(8,128)S(1)} %get-tuple-element.39), channel_id=1, source_target_pairs={{0,32},{1,33},{2,34},{3,35},{4,36},{5,37},{6,38},{7,39},{64,96},{6... | collective-permute-start | bytes 393224 | tf_op jit(solution)/shard_map/ppermute | solution.py:122
  72.0 15.4 %collective-permute-start.10 = (f32[64,512]{1,0:T(8,128)S(1)}, f32[64,512]{1,0:T(8,128)}, u32[]{:S(2)}, u32[]{:S(2)}) collective-permute-start(f32[64,512]{1,0:T(8,128)S(1)} %get-tuple-element.40), channel_id=1, source_target_pairs={{0,40},{1,41},{2,42},{3,43},{4,44},{5,45},{6,46},{7,47},{64,104},{... | collective-permute-start | bytes 393224 | tf_op jit(solution)/shard_map/ppermute | solution.py:122
  73.3 14.1 %collective-permute-start.9 = (f32[64,512]{1,0:T(8,128)S(1)}, f32[64,512]{1,0:T(8,128)}, u32[]{:S(2)}, u32[]{:S(2)}) collective-permute-start(f32[64,512]{1,0:T(8,128)S(1)} %get-tuple-element.41), channel_id=1, source_target_pairs={{0,48},{1,49},{2,50},{3,51},{4,52},{5,53},{6,54},{7,55},{64,112},{... | collective-permute-start | bytes 393224 | tf_op jit(solution)/shard_map/ppermute | solution.py:122
  74.7 12.8 %collective-permute-start.8 = (f32[64,512]{1,0:T(8,128)S(1)}, f32[64,512]{1,0:T(8,128)}, u32[]{:S(2)}, u32[]{:S(2)}) collective-permute-start(f32[64,512]{1,0:T(8,128)S(1)} %get-tuple-element.42), channel_id=1, source_target_pairs={{0,56},{1,57},{2,58},{3,59},{4,60},{5,61},{6,62},{7,63},{64,120},{... | collective-permute-start | bytes 393224 | tf_op jit(solution)/shard_map/ppermute | solution.py:122
  76.0 15.5 %collective-permute-start.7 = (f32[128,512]{1,0:T(8,128)S(1)}, f32[128,512]{1,0:T(8,128)S(1)}, u32[]{:S(2)}, u32[]{:S(2)}) collective-permute-start(f32[128,512]{1,0:T(8,128)S(1)} %constant_dynamic-slice_fusion), channel_id=1, source_target_pairs={{0,0},{1,8},{2,16},{3,24},{4,32},{5,40},{6,48},{7,56},{8,1},{9,9},... | collective-permute-start | bytes 786440 | tf_op jit(solution)/shard_map/ppermute | solution.py:118
  210.7 30.2 %copy-start.5 = (f32[8,128,512]{2,1,0:T(8,128)S(1)}, f32[8,128,512]{2,1,0:T(8,128)}, u32[]{:S(2)}) copy-start(f32[8,128,512]{2,1,0:T(8,128)} %slice.219) | copy-start | bytes 6291460
  237.7 9.2 %copy-start.20 = (f32[128,128]{1,0:T(8,128)}, f32[128,128]{1,0:T(8,128)S(1)}, u32[]{:S(2)}) copy-start(f32[128,128]{1,0:T(8,128)S(1)} %copy.51) | copy-start | bytes 196612
  238.3 8.6 %copy-start.15 = (f32[128,128]{1,0:T(8,128)}, f32[128,128]{1,0:T(8,128)S(1)}, u32[]{:S(2)}) copy-start(f32[128,128]{1,0:T(8,128)S(1)} %convolution_negate_fusion.2) | copy-start | bytes 196612
  238.6 8.3 %copy-start.16 = (f32[128,128]{1,0:T(8,128)}, f32[128,128]{1,0:T(8,128)S(1)}, u32[]{:S(2)}) copy-start(f32[128,128]{1,0:T(8,128)S(1)} %convolution_negate_fusion) | copy-start | bytes 196612
  239.5 7.5 %copy-start.17 = (f32[128,128]{1,0:T(8,128)}, f32[128,128]{1,0:T(8,128)S(1)}, u32[]{:S(2)}) copy-start(f32[128,128]{1,0:T(8,128)S(1)} %convolution_negate_fusion.1) | copy-start | bytes 196612
  241.0 6.1 %copy-start.3 = (f32[8,128,512]{2,1,0:T(8,128)S(1)}, f32[8,128,512]{2,1,0:T(8,128)}, u32[]{:S(2)}) copy-start(f32[8,128,512]{2,1,0:T(8,128)} %copy-done.2) | copy-start | bytes 6291460
  241.0 6.1 %copy-start.18 = (f32[128,128]{1,0:T(8,128)S(1)}, f32[128,128]{1,0:T(8,128)}, u32[]{:S(2)}) copy-start(f32[128,128]{1,0:T(8,128)} %copy.44) | copy-start | bytes 196612
  241.0 6.1 %copy-start.19 = (f32[128,128]{1,0:T(8,128)S(1)}, f32[128,128]{1,0:T(8,128)}, u32[]{:S(2)}) copy-start(f32[128,128]{1,0:T(8,128)} %copy.47) | copy-start | bytes 196612
  241.1 6.1 %copy-start.21 = (pred[1024]{0:T(1024)(128)(4,1)S(1)}, pred[1024]{0:T(1024)(128)(4,1)}, u32[]{:S(2)}) copy-start(pred[1024]{0:T(1024)(128)(4,1)} %get-tuple-element.60) | copy-start | bytes 3076
  257.0 9.9 %copy-start.4 = (f32[1024,1024]{1,0:T(8,128)S(1)}, f32[1024,1024]{1,0:T(8,128)}, u32[]{:S(2)}) copy-start(f32[1024,1024]{1,0:T(8,128)} %gather_fusion.1) | copy-start | bytes 12582916
  257.0 9.9 %copy-start.23 = (pred[1024]{0:T(1024)(128)(4,1)S(1)}, pred[1024]{0:T(1024)(128)(4,1)}, u32[]{:S(2)}) copy-start(pred[1024]{0:T(1024)(128)(4,1)} %fusion.92) | copy-start | bytes 3076
  257.0 9.9 %copy-start.24 = (s32[1024]{0:T(1024)S(1)}, s32[1024]{0:T(1024)}, u32[]{:S(2)}) copy-start(s32[1024]{0:T(1024)} %get-tuple-element.11) | copy-start | bytes 12292
  279.8 10.7 %copy-start.14 = (s32[2,8192]{1,0:T(2,128)S(1)}, s32[2,8192]{1,0:T(2,128)}, u32[]{:S(2)}) copy-start(s32[2,8192]{1,0:T(2,128)} %param.11) | copy-start | bytes 196612
  279.8 65.7 %all-to-all-start.1 = ((f32[128,64,128]{2,1,0:T(8,128)}), f32[128,64,128]{2,1,0:T(8,128)}, u32[]{:S(2)}, u32[]{:S(2)}) async-start(f32[128,64,128]{2,1,0:T(8,128)} %bitcast.122), calls=%async_computation.1 | async-start | bytes 8388608 | tf_op jit(solution)/shard_map/all_to_all | solution.py:155
  (11 other events, 60.6 us)
Sparse Core Ops, SparseCore 0:
  92.4 35.2 all-gather.2
